TPU v7x, 512 devices: a whole 4x8x8 slice. The times are simulated.
512 devices in a mesh: slab: 64 (over z, x, core), obs: 8 (over y).
Axes of the slice: x: 4, y: 8, z: 8, core: 2. Of those that a mesh axis runs over, the one named last changes fastest.
Arguments:
- background_members: float32 [64, 1048576], P('slab', 'obs'), may hold values from -6 to 6
- measurement_jitter: bfloat16 [64, 8, 65536], P(None, 'obs', 'slab'), may hold values from -5 to 5
- measurement_readings: float32 [8, 65536], P('obs', 'slab'), may hold values from -8 to 8
- measurement_noise_spread: float32 [8, 65536], P('obs', 'slab'), may hold values from 0.2 to 2
- measurement_grid_location: int32 [8, 65536], P('obs', 'slab'), may hold values from 0 to 2047
- active_tallies: int32 [8, 64], P('obs', 'slab'), may hold values from 128 to 1024, as said below
- coupling_listing: int32 [8, 2048, 8], P('obs', 'slab'), may hold values from 0 to 63, as said below
- taper_factors: float32 [8, 2048, 8], P('obs', 'slab'), may hold values from 0.1 to 1
Outputs:
- analysis: float32 [64, 1048576], P('slab', 'obs')
Inputs may be any that keep to these rules, and one draw needn't show every extreme that they name: `active_tallies`: some region of some group holds 1024 live observations; slots beyond a region's count are padding. `coupling_listing`: the 8 observation blocks listed for a state block are distinct.
All inputs are finite; a program needn't handle non-finite values.
Results may differ from a plain program's by a relative error of at most 0.0063.
Values may be sent and summed in bfloat16 or wider, within the bound.
No kernel may reach another device: no remote copies, remote signals or barrier semaphores. Data moves between devices by JAX's collectives and lax.ppermute only.
A program may use at most 64 MiB of HBM per device.

v0:
```python
import jax
import jax.numpy as jnp
from jax import lax
from jax.sharding import PartitionSpec as P

OB = 128
highest = lax.Precision.HIGHEST


def block_products(
    tile_work,
    measurement_jitter,
    measurement_readings,
    measurement_noise_spread,
    measurement_grid_location,
    active_tallies,
):
    members = tile_work.shape[0]
    positions = measurement_grid_location[0]
    obs_count = positions.shape[0]
    prior_value = jnp.take(tile_work, positions, axis=1)
    prior_shift = prior_value - jnp.mean(prior_value, axis=0, keepdims=True)
    spread = jnp.sum(prior_shift * prior_shift, axis=0, keepdims=True) / (members - 1)
    usable = jnp.arange(obs_count, dtype=jnp.int32)[None, :] < active_tallies[0, 0]
    innovation = (
        measurement_readings + measurement_jitter[:, 0, :].astype(jnp.float32) - prior_value
    ) / (spread + measurement_noise_spread)
    gain_input = jnp.where(usable, innovation, jnp.float32(0.0)).astype(jnp.bfloat16)
    prior_low = prior_shift.astype(jnp.bfloat16)
    return jnp.einsum(
        "mco,nco->cmn",
        gain_input.reshape(members, -1, OB),
        prior_low.reshape(members, -1, OB),
        preferred_element_type=jnp.float32,
    )


def local(
    background_members,
    measurement_jitter,
    measurement_readings,
    measurement_noise_spread,
    measurement_grid_location,
    active_tallies,
    coupling_listing,
    taper_factors,
):
    work_low = background_members.astype(jnp.bfloat16)
    tile_low = lax.all_to_all(work_low, "slab", split_axis=1, concat_axis=0, tiled=True)
    tile_work = tile_low.astype(jnp.float32)
    members = tile_work.shape[0]
    blocks = coupling_listing.shape[1]
    deviation = tile_work - jnp.mean(tile_work, axis=0, keepdims=True)
    products = block_products(
        tile_work,
        measurement_jitter,
        measurement_readings,
        measurement_noise_spread,
        measurement_grid_location,
        active_tallies,
    )
    all_products = lax.all_gather(products, "obs", axis=0, tiled=True)
    obs_blocks = all_products.shape[0]
    block_links = coupling_listing[0]
    factor = taper_factors[0] / (members - 1)
    choose = block_links[..., None] == jnp.arange(obs_blocks, dtype=jnp.int32)
    localize = jnp.sum(jnp.where(choose, factor[..., None], jnp.float32(0.0)), axis=1)
    ensemble = jnp.einsum("bc,cmn->bmn", localize, all_products, precision=highest)
    region_dev = deviation.reshape(members, blocks, -1)
    increment = jnp.einsum("bmn,nbp->mbp", ensemble, region_dev, precision=highest)
    increment_low = increment.reshape(members, -1).astype(jnp.bfloat16)
    back = lax.all_to_all(increment_low, "slab", split_axis=0, concat_axis=1, tiled=True)
    return background_members + back.astype(jnp.float32)


def solution(mesh):
    return jax.shard_map(
        local,
        mesh=mesh,
        in_specs=(
            P("slab", "obs"),
            P(None, "obs", "slab"),
            P("obs", "slab"),
            P("obs", "slab"),
            P("obs", "slab"),
            P("obs", "slab"),
            P("obs", "slab", None),
            P("obs", "slab", None),
        ),
        out_specs=P("slab", "obs"),
        check_vma=False,
    )
```

profile of v0, /device:TPU:1, one launch (start us, length us, event | category | flops | bytes accessed | tf_op | source)
XLA Modules:
  0.0 124.3 jit_solution(9766494422847316278)
XLA Ops:
  6.5 0.0 copy-start.1
  6.5 0.0 copy-start.2
  6.5 1.4 %convert_element_type.60 = bf16[1,131072]{1,0:T(2,128)(2,1)S(1)} convert(f32[1,131072]{1,0:T(1,128)} %param.8) | non-fusion elementwise | flops 131072 | bytes 786432 | tf_op jit(solution)/shard_map/convert_element_type | solution.py:48
  8.0 0.5 broadcast.91
  8.5 2.1 %reduce.1 = bf16[64,2048]{1,0:T(8,128)(2,1)S(1)} reduce(bf16[64,1,2048]{2,1,0:T(2,128)(2,1)S(1)} %bitcast.46, bf16[]{:T(256)} %broadcast.91), dimensions={1}, to_apply=%bitcast.40.reduce_sub_computation | reduce | bytes 524290
  10.6 0.9 reshape.167
  11.5 14.8 %all-to-all-start = ((bf16[64,2,1024]{2,1,0:T(2,128)(2,1)}), bf16[64,2,1024]{2,1,0:T(2,128)(2,1)S(1)}, u32[]{:S(2)}, u32[]{:S(2)}) async-start(bf16[64,2,1024]{2,1,0:T(2,128)(2,1)} %reshape.167), calls=%async_computation | async-start | bytes 524288 | tf_op jit(solution)/shard_map/all_to_all | solution.py:49
  26.3 0.0 all-gather.2.cloned.1.call-start
  27.0 0.0 copy-done.1
  27.1 0.0 copy-done.2
  27.2 12.2 %all-to-all-done = bf16[64,2,1024]{2,1,0:T(2,128)(2,1)S(1)} async-done(((bf16[64,2,1024]{2,1,0:T(2,128)(2,1)}), bf16[64,2,1024]{2,1,0:T(2,128)(2,1)S(1)}, u32[]{:S(2)}, u32[]{:S(2)}) %all-to-all-start) | async-done | bytes 262176 | tf_op jit(solution)/shard_map/all_to_all | solution.py:49
  39.4 0.2 reshape.168
  39.7 0.5 copy.28
  40.2 0.1 convert_bitcast_fusion
  40.3 0.0 copy-start.3
  40.3 0.0 copy-start.6
  40.3 2.8 %gather_fusion = f32[1024,64]{1,0:T(8,128)S(1)} fusion(f32[64,2048]{0,1:T(8,128)S(1)} %convert_bitcast_fusion, s32[1024]{0:T(1024)S(1)} %broadcast_clamp_fusion), kind=kCustom, calls=%fused_computation | custom fusion | bytes 528384 | tf_op jit(solution)/shard_map/jit(_take)/gather | solution.py:21
  43.1 0.0 copy-start.5
  43.1 0.0 copy-start.4
  43.1 0.4 fusion.5
  43.5 0.5 multiply_reduce_fusion
  44.0 0.2 copy.32
  44.2 0.0 copy-done.3
  44.2 0.0 copy-done.6
  44.2 0.9 fusion.10
  45.2 0.0 all-gather.2.cloned.1.call-update
  45.2 0.0 copy-done.5
  45.2 0.1 copy.30
  45.3 0.0 copy-done.4
  45.3 0.1 copy.29
  45.4 0.1 select_reduce_fusion
  45.5 0.2 convert_reduce_fusion
  45.7 0.1 div.45
  45.8 34.1 %all-gather.2.cloned.1.call-done = f32[64,64,64]{2,1,0:T(8,128)} async-done(((f32[8,64,64]{2,1,0:T(8,128)}), f32[64,64,64]{2,1,0:T(8,128)}) %all-gather.2.cloned.1.call-update) | async-done | bytes 1048592 | tf_op jit(solution)/shard_map/all_gather | solution.py:62
  80.0 3.9 %fusion = f32[32,64,64]{2,0,1:T(8,128)S(1)} fusion(f32[64,64,64]{2,1,0:T(8,128)} %all-gather.2.cloned.1.call-done, f32[32,64]{1,0:T(8,128)S(1)} %select_reduce_fusion), kind=kOutput, calls=%fused_computation.1 | convolution fusion | flops 100663296 | bytes 1581056 | tf_op jit(solution)/shard_map/bc,cmn->bmn/dot_general | solution.py:68
  83.8 2.3 %convolution_convert_fusion = bf16[32,64,64]{2,1,0:T(8,128)(2,1)S(1)} fusion(f32[32,64,64]{2,0,1:T(8,128)S(1)} %fusion, f32[32,64]{1,0:T(8,128)S(1)} %div.45, bf16[64,32,64]{0,2,1:T(8,128)(2,1)S(1)} %bitcast.43), kind=kOutput, calls=%fused_computation.3 | convolution fusion | flops 101056512 | bytes 1056768 | tf_op jit(solution)/shard_map/bmn,nbp->mbp/dot_general | solution.py:70
  86.2 0.0 copy-start
  86.2 1.1 reduce.2
  87.3 0.2 copy.51
  87.5 0.2 reshape.169
  87.7 28.1 %all_to_all.23 = bf16[64,2,1024]{2,1,0:T(2,128)(2,1)S(1)} all-to-all(bf16[64,2,1024]{2,1,0:T(2,128)(2,1)S(1)} %reshape.169), channel_id=1, replica_groups=mesh['slab'=64,'obs'=8] {'slab'}, dimensions={0} | all-to-all | bytes 524288 | tf_op jit(solution)/shard_map/all_to_all | solution.py:72
  115.8 0.2 reshape.170
  116.0 0.0 copy-done
  116.0 1.5 %convert_add_fusion = f32[1,131072]{1,0:T(1,128)} fusion(f32[1,131072]{1,0:T(1,128)S(1)} %copy-done, bf16[1,131072]{1,0:T(2,128)(2,1)S(1)} %bitcast.45), kind=kLoop, calls=%fused_computation.6 | loop fusion | flops 262144 | bytes 1310720 | tf_op jit(solution)/shard_map/add | solution.py:73
  (11 shorter events, 0.1 us)
Async XLA Ops:
  6.5 20.5 %copy-start.1 = (bf16[64,1,1024]{2,0,1:T(8,128)(2,1)S(1)}, bf16[64,1,1024]{2,0,1:T(8,128)(2,1)}, u32[]{:S(2)}) copy-start(bf16[64,1,1024]{2,0,1:T(8,128)(2,1)} %param.9) | copy-start | bytes 393220
  6.5 20.5 %copy-start.2 = (s32[1,1024]{1,0:T(1,128)S(1)}, s32[1,1024]{1,0:T(1,128)}, u32[]{:S(2)}) copy-start(s32[1,1024]{1,0:T(1,128)} %param.12) | copy-start | bytes 12292
  11.5 27.9 %all-to-all-start = ((bf16[64,2,1024]{2,1,0:T(2,128)(2,1)}), bf16[64,2,1024]{2,1,0:T(2,128)(2,1)S(1)}, u32[]{:S(2)}, u32[]{:S(2)}) async-start(bf16[64,2,1024]{2,1,0:T(2,128)(2,1)} %reshape.167), calls=%async_computation | async-start | bytes 524288 | tf_op jit(solution)/shard_map/all_to_all | solution.py:49
  26.3 53.6 %all-gather.2.cloned.1.call-start = ((), (), s32[]{:S(2)}) async-start(), calls=%async_computation.2 | async-start | bytes 2359296 | tf_op jit(solution)/shard_map/all_gather | solution.py:62
  40.3 4.0 %copy-start.3 = (f32[1,1024]{1,0:T(1,128)S(1)}, f32[1,1024]{1,0:T(1,128)}, u32[]{:S(2)}) copy-start(f32[1,1024]{1,0:T(1,128)} %param.11) | copy-start | bytes 12292
  40.3 4.0 %copy-start.6 = (f32[1,1024]{1,0:T(1,128)S(1)}, f32[1,1024]{1,0:T(1,128)}, u32[]{:S(2)}) copy-start(f32[1,1024]{1,0:T(1,128)} %param.10) | copy-start | bytes 12292
  43.1 2.1 %copy-start.5 = (f32[1,32,8]{1,2,0:T(8,128)S(1)}, f32[1,32,8]{1,2,0:T(8,128)}, u32[]{:S(2)}) copy-start(f32[1,32,8]{1,2,0:T(8,128)} %param.15) | copy-start | bytes 3076
  43.1 2.2 %copy-start.4 = (s32[1,32,8]{1,2,0:T(8,128)S(1)}, s32[1,32,8]{1,2,0:T(8,128)}, u32[]{:S(2)}) copy-start(s32[1,32,8]{1,2,0:T(8,128)} %param.14) | copy-start | bytes 3076
  86.2 29.8 %copy-start = (f32[1,131072]{1,0:T(1,128)S(1)}, f32[1,131072]{1,0:T(1,128)}, u32[]{:S(2)}) copy-start(f32[1,131072]{1,0:T(1,128)} %param.8) | copy-start | bytes 1572868
Sparse Core Ops, SparseCore 0:
  45.3 34.6 all-gather.1
where the time goes:
time: 125 us; the launch traced here: 124 us
  waiting for transfers between devices  46.4 us (37%)
  blocking collectives  28.1 us (22%)
  starting transfers between devices  14.9 us (12%)
  between operations  14.3 us (11%)
  other arithmetic  7.54 us (6%)
  matrix products  7.11 us (6%)
  local copies, waits for them, and re-layouts  6.04 us (5%)
    all_gather x1, waiting for transfers between devices, local(): all_products = lax.all_gather(products, 'obs', axis=0, tiled=True)  34.1 us
    all_to_all x1, blocking collectives, local(): lax.all_to_all(increment_low, 'slab', split_axis=0, concat_axis=1, tiled=...  28.1 us
    all_to_all x1, starting transfers between devices, local(): lax.all_to_all(work_low, 'slab', split_axis=1, concat_axis=0, tiled=True)  14.8 us
    all_to_all x1, waiting for transfers between devices, local(): lax.all_to_all(work_low, 'slab', split_axis=1, concat_axis=0, tiled=True)  12.2 us
    dot_general x1, matrix products, local(): jnp.einsum('bc,cmn->bmn', localize, all_products, precision=highest)  3.85 us
    gather x2, local copies, waits for them, and re-layouts, block_products(): prior_value = jnp.take(tile_work, positions, axis=1)  2.99 us
  transfers between devices with their start and end apart: 2, of which 2 were waited for; matrix products, arithmetic and copies ran while one was open for 1% of the time, Pallas kernels for 0%

commit v1 on v0

--- a/solution.py
+++ b/solution.py
@@ -59,7 +59,9 @@
         measurement_grid_location,
         active_tallies,
     )
-    all_products = lax.all_gather(products, "obs", axis=0, tiled=True)
+    all_products = jnp.concatenate(
+        lax.all_to_all(jnp.stack(lax.axis_size("obs") * [products]), "obs", 0, 0), axis=0
+    )
     obs_blocks = all_products.shape[0]
     block_links = coupling_listing[0]
     factor = taper_factors[0] / (members - 1)

time: 125 us -> 108 us (0.86)
  between operations: 14.3 us -> 0.95 us
  blocking collectives: 28.1 us -> 17.6 us
  starting transfers between devices: 14.9 us -> 21.6 us
  waiting for transfers between devices: 46.4 us -> 40.9 us
  local copies, waits for them, and re-layouts: 6.04 us -> 11.1 us
  other arithmetic: 7.54 us -> 12.2 us
  matrix products: 7.11 us -> 3.67 us
    all_gather x1 -> x0, waiting for transfers between devices: 34.1 us -> none  [local(): all_products = lax.all_gather(products, 'obs', axis=0, tiled=True)]
    all_to_all x0 -> x1, waiting for transfers between devices: none -> 28.6 us  [local(): lax.all_to_all(jnp.stack(lax.axis_size('obs') * [products]), 'obs', 0, 0)]
    all_to_all x1, blocking collectives: 28.1 us -> 17.6 us  [local(): lax.all_to_all(increment_low, 'slab', split_axis=0, concat_axis=1, tiled=...]
    all_to_all x0 -> x1, starting transfers between devices: none -> 6.82 us  [local(): lax.all_to_all(jnp.stack(lax.axis_size('obs') * [products]), 'obs', 0, 0)]
    all_to_all x0 -> x1, other arithmetic: none -> 4.52 us  [local(): lax.all_to_all(jnp.stack(lax.axis_size('obs') * [products]), 'obs', 0, 0)]
    unnamed x21 -> x24, local copies, waits for them, and re-layouts: 2.31 us -> 6.72 us
    dot_general x1, matrix products: 3.85 us -> 1.11 us  [local(): jnp.einsum('bc,cmn->bmn', localize, all_products, precision=highest)]
where the time goes in v1:
time: 108 us
  waiting for transfers between devices  40.9 us (38%)
  starting transfers between devices  21.6 us (20%)
  blocking collectives  17.6 us (16%)
  other arithmetic  12.2 us (11%)
  local copies, waits for them, and re-layouts  11.1 us (10%)
  matrix products  3.67 us (3%)
    all_to_all x1, waiting for transfers between devices, local(): lax.all_to_all(jnp.stack(lax.axis_size('obs') * [products]), 'obs', 0, 0)  28.6 us
    all_to_all x1, blocking collectives, local(): lax.all_to_all(increment_low, 'slab', split_axis=0, concat_axis=1, tiled=...  17.6 us
    all_to_all x1, starting transfers between devices, local(): lax.all_to_all(work_low, 'slab', split_axis=1, concat_axis=0, tiled=True)  14.8 us
    all_to_all x1, waiting for transfers between devices, local(): lax.all_to_all(work_low, 'slab', split_axis=1, concat_axis=0, tiled=True)  12.3 us
    all_to_all x1, starting transfers between devices, local(): lax.all_to_all(jnp.stack(lax.axis_size('obs') * [products]), 'obs', 0, 0)  6.82 us
    unnamed x24, local copies, waits for them, and re-layouts  6.72 us
    all_to_all x1, other arithmetic, local(): lax.all_to_all(jnp.stack(lax.axis_size('obs') * [products]), 'obs', 0, 0)  4.52 us
    gather x2, local copies, waits for them, and re-layouts, block_products(): prior_value = jnp.take(tile_work, positions, axis=1)  2.99 us
  transfers between devices with their start and end apart: 2, of which 2 were waited for; matrix products, arithmetic and copies ran while one was open for 1% of the time, Pallas kernels for 0%

profile of v1, /device:TPU:1, one launch (start us, length us, event | category | flops | bytes accessed | tf_op | source)
XLA Modules:
  0.0 108.1 jit_solution(8541478088746418677)
XLA Ops:
  0.0 0.0 copy-start.1
  0.0 1.4 %convert_element_type.60 = bf16[1,131072]{1,0:T(2,128)(2,1)S(1)} convert(f32[1,131072]{1,0:T(1,128)} %param.8) | non-fusion elementwise | flops 131072 | bytes 786432 | tf_op jit(solution)/shard_map/convert_element_type | solution.py:48
  1.4 0.6 broadcast.93
  2.0 2.2 %reduce.1 = bf16[64,2048]{1,0:T(8,128)(2,1)S(1)} reduce(bf16[64,1,2048]{2,1,0:T(2,128)(2,1)S(1)} %bitcast.55, bf16[]{:T(256)} %broadcast.93), dimensions={1}, to_apply=%bitcast.43.reduce_sub_computation | reduce | bytes 524290
  4.2 0.9 reshape.173
  5.1 14.8 %all-to-all-start = ((bf16[64,2,1024]{2,1,0:T(2,128)(2,1)}), bf16[64,2,1024]{2,1,0:T(2,128)(2,1)S(1)}, u32[]{:S(2)}, u32[]{:S(2)}) async-start(bf16[64,2,1024]{2,1,0:T(2,128)(2,1)} %reshape.173), calls=%async_computation | async-start | bytes 524288 | tf_op jit(solution)/shard_map/all_to_all | solution.py:49
  20.6 0.0 copy-done.1
  20.6 0.0 copy-done.2
  20.8 12.3 %all-to-all-done = bf16[64,2,1024]{2,1,0:T(2,128)(2,1)S(1)} async-done(((bf16[64,2,1024]{2,1,0:T(2,128)(2,1)}), bf16[64,2,1024]{2,1,0:T(2,128)(2,1)S(1)}, u32[]{:S(2)}, u32[]{:S(2)}) %all-to-all-start) | async-done | bytes 262176 | tf_op jit(solution)/shard_map/all_to_all | solution.py:49
  33.0 0.2 reshape.174
  33.3 0.5 copy.40
  33.8 0.1 convert_bitcast_fusion
  33.9 0.0 copy-start.3
  33.9 0.0 copy-start.6
  33.9 2.8 %gather_fusion = f32[1024,64]{1,0:T(8,128)S(1)} fusion(f32[64,2048]{0,1:T(8,128)S(1)} %convert_bitcast_fusion, s32[1024]{0:T(1024)S(1)} %broadcast_clamp_fusion), kind=kCustom, calls=%fused_computation | custom fusion | bytes 528384 | tf_op jit(solution)/shard_map/jit(_take)/gather | solution.py:21
  36.7 0.4 fusion.6
  37.1 0.5 multiply_reduce_fusion
  37.6 0.2 copy.44
  37.8 0.0 copy-done.3
  37.8 0.0 copy-done.6
  37.8 0.2 fusion.11
  38.0 0.2 copy.45
  38.2 0.1 broadcast_bitcast_fusion
  38.4 0.0 copy-start.5
  38.4 0.0 copy-start.4
  38.4 2.1 %reshape.175 = f32[8,1,32768]{2,1,0:T(1,128)} reshape(f32[8,64,8,64]{3,2,1,0:T(8,128)S(1)} %broadcast_bitcast_fusion) | data formatting | bytes 2097152
  40.5 6.8 %all-to-all-start.1 = ((f32[8,1,32768]{2,1,0:T(1,128)}), f32[8,1,32768]{2,1,0:T(1,128)S(1)}, u32[]{:S(2)}, u32[]{:S(2)}) async-start(f32[8,1,32768]{2,1,0:T(1,128)} %reshape.175), calls=%async_computation.1 | async-start | bytes 2097152 | tf_op jit(solution)/shard_map/all_to_all | solution.py:63
  47.3 0.0 copy-done.5
  47.4 0.1 copy.42
  47.4 0.0 copy-done.4
  47.4 0.1 copy.41
  47.5 0.1 select_reduce_fusion
  47.7 0.2 convert_reduce_fusion
  47.9 0.1 div.45
  48.0 28.6 %all-to-all-done.1 = f32[8,1,32768]{2,1,0:T(1,128)S(1)} async-done(((f32[8,1,32768]{2,1,0:T(1,128)}), f32[8,1,32768]{2,1,0:T(1,128)S(1)}, u32[]{:S(2)}, u32[]{:S(2)}) %all-to-all-start.1) | async-done | bytes 1048608 | tf_op jit(solution)/shard_map/all_to_all | solution.py:63
  76.6 0.5 broadcast.94
  77.1 4.5 %reduce.2 = f32[8,32768]{1,0:T(8,128)} reduce(f32[8,1,32768]{2,1,0:T(1,128)S(1)} %all-to-all-done.1, f32[]{:T(128)} %broadcast.94), dimensions={1}, to_apply=%all_to_all.23.reduce_sub_computation | reduce | bytes 2097156 | tf_op jit(solution)/shard_map/all_to_all | solution.py:63
  81.6 2.1 %reshape.176 = f32[8,64,8,64]{3,2,1,0:T(8,128)S(1)} reshape(f32[8,32768]{1,0:T(8,128)} %reduce.2) | data formatting | bytes 2097152
  83.7 1.1 %fusion = f32[32,64,64]{2,0,1:T(8,128)S(1)} fusion(f32[32,64]{1,0:T(8,128)S(1)} %select_reduce_fusion, f32[8,64,8,64]{3,2,1,0:T(8,128)S(1)} %reshape.176), kind=kOutput, calls=%fused_computation.1 | convolution fusion | flops 100663296 | bytes 1581056 | tf_op jit(solution)/shard_map/bc,cmn->bmn/dot_general | solution.py:70
  84.8 2.3 %convolution_convert_fusion = bf16[32,64,64]{2,1,0:T(8,128)(2,1)S(1)} fusion(f32[32,64,64]{2,0,1:T(8,128)S(1)} %fusion, f32[32,64]{1,0:T(8,128)S(1)} %div.45, bf16[64,32,64]{0,2,1:T(8,128)(2,1)S(1)} %bitcast.52), kind=kOutput, calls=%fused_computation.4 | convolution fusion | flops 101056512 | bytes 1056768 | tf_op jit(solution)/shard_map/bmn,nbp->mbp/dot_general | solution.py:72
  87.2 0.0 copy-start
  87.2 1.2 %reduce.3 = bf16[64,2048]{0,1:T(8,128)(2,1)S(1)} reduce(bf16[64,1,2048]{0,2,1:T(8,128)(2,1)S(1)} %bitcast.57, bf16[]{:T(256)} %broadcast.93), dimensions={1}, to_apply=%copy.48.reduce_sub_computation | reduce | bytes 524290 | tf_op jit(solution)/shard_map/convert_element_type | solution.py:73
  88.4 0.2 copy.66
  88.6 0.2 reshape.177
  88.8 17.6 %all_to_all.28 = bf16[64,2,1024]{2,1,0:T(2,128)(2,1)S(1)} all-to-all(bf16[64,2,1024]{2,1,0:T(2,128)(2,1)S(1)} %reshape.177), channel_id=1, replica_groups=mesh['slab'=64,'obs'=8] {'slab'}, dimensions={0} | all-to-all | bytes 524288 | tf_op jit(solution)/shard_map/all_to_all | solution.py:74
  106.4 0.2 reshape.178
  106.6 0.0 copy-done
  106.6 1.5 %convert_add_fusion = f32[1,131072]{1,0:T(1,128)} fusion(f32[1,131072]{1,0:T(1,128)S(1)} %copy-done, bf16[1,131072]{1,0:T(2,128)(2,1)S(1)} %bitcast.54), kind=kLoop, calls=%fused_computation.7 | loop fusion | flops 262144 | bytes 1310720 | tf_op jit(solution)/shard_map/add | solution.py:75
  (12 shorter events, 0.1 us)
Async XLA Ops:
  0.0 20.6 %copy-start.1 = (bf16[64,1,1024]{2,0,1:T(8,128)(2,1)S(1)}, bf16[64,1,1024]{2,0,1:T(8,128)(2,1)}, u32[]{:S(2)}) copy-start(bf16[64,1,1024]{2,0,1:T(8,128)(2,1)} %param.9) | copy-start | bytes 393220
  0.0 20.6 %copy-start.2 = (s32[1,1024]{1,0:T(1,128)S(1)}, s32[1,1024]{1,0:T(1,128)}, u32[]{:S(2)}) copy-start(s32[1,1024]{1,0:T(1,128)} %param.12) | copy-start | bytes 12292
  5.1 27.9 %all-to-all-start = ((bf16[64,2,1024]{2,1,0:T(2,128)(2,1)}), bf16[64,2,1024]{2,1,0:T(2,128)(2,1)S(1)}, u32[]{:S(2)}, u32[]{:S(2)}) async-start(bf16[64,2,1024]{2,1,0:T(2,128)(2,1)} %reshape.173), calls=%async_computation | async-start | bytes 524288 | tf_op jit(solution)/shard_map/all_to_all | solution.py:49
  33.9 3.9 %copy-start.3 = (f32[1,1024]{1,0:T(1,128)S(1)}, f32[1,1024]{1,0:T(1,128)}, u32[]{:S(2)}) copy-start(f32[1,1024]{1,0:T(1,128)} %param.11) | copy-start | bytes 12292
  33.9 3.9 %copy-start.6 = (f32[1,1024]{1,0:T(1,128)S(1)}, f32[1,1024]{1,0:T(1,128)}, u32[]{:S(2)}) copy-start(f32[1,1024]{1,0:T(1,128)} %param.10) | copy-start | bytes 12292
  38.4 9.0 %copy-start.5 = (f32[1,32,8]{1,2,0:T(8,128)S(1)}, f32[1,32,8]{1,2,0:T(8,128)}, u32[]{:S(2)}) copy-start(f32[1,32,8]{1,2,0:T(8,128)} %param.15) | copy-start | bytes 3076
  38.4 9.1 %copy-start.4 = (s32[1,32,8]{1,2,0:T(8,128)S(1)}, s32[1,32,8]{1,2,0:T(8,128)}, u32[]{:S(2)}) copy-start(s32[1,32,8]{1,2,0:T(8,128)} %param.14) | copy-start | bytes 3076
  40.5 36.1 %all-to-all-start.1 = ((f32[8,1,32768]{2,1,0:T(1,128)}), f32[8,1,32768]{2,1,0:T(1,128)S(1)}, u32[]{:S(2)}, u32[]{:S(2)}) async-start(f32[8,1,32768]{2,1,0:T(1,128)} %reshape.175), calls=%async_computation.1 | async-start | bytes 2097152 | tf_op jit(solution)/shard_map/all_to_all | solution.py:63
  87.2 19.4 %copy-start = (f32[1,131072]{1,0:T(1,128)S(1)}, f32[1,131072]{1,0:T(1,128)}, u32[]{:S(2)}) copy-start(f32[1,131072]{1,0:T(1,128)} %param.8) | copy-start | bytes 1572868
